TPU v7x, 256 devices: a whole 4x4x8 slice. The times are simulated.
256 devices in a mesh: wide: 64 (over z, x, y_lo), narrow: 4 (over y_hi, core).
Axes of the slice: x: 4, y: 4 (y_hi: 2, y_lo: 2; y = y_hi * 2 + y_lo), z: 8, core: 2. Of those that a mesh axis runs over, the one named last changes fastest.
Arguments:
- density: bfloat16 [8192, 8, 128], P(('wide', 'narrow')), may hold values from -6 to 6
- basis: bfloat16 [8192, 64, 128], P(('wide', 'narrow')), may hold values from -0.5 to 0.5
- near_list: int32 [8192, 6], P(('wide', 'narrow')), may hold values from 0 to 8191, as said below
- near_blocks: bfloat16 [8192, 6, 128, 128], P(('wide', 'narrow')), may hold values from -0.21875 to 0.21875
- far_leaf: int32 [8192, 6], P(('wide', 'narrow')), may hold values from 0 to 8191, as said below
- leaf_coupling: bfloat16 [8192, 64, 384], P(('wide', 'narrow')), may hold values from -0.3125 to 0.3125
- transfer: bfloat16 [1024, 64, 512], P(('wide', 'narrow')), may hold values from -0.75 to 0.75
- far_coarse: int32 [1024, 8], P(('wide', 'narrow')), may hold values from 0 to 1023
- coarse_coupling: bfloat16 [1024, 64, 512], P(('wide', 'narrow')), may hold values from -0.25 to 0.25
Outputs:
- potential: bfloat16 [8192, 8, 128], P(('wide', 'narrow'))
Inputs may be any that keep to these rules, and one draw needn't show every extreme that they name: `near_list`: every entry lies within 32 leaves of its own leaf l; the first entry is l itself. `far_leaf`: every entry lies within 32 leaves of its own leaf.
All inputs are finite; a program needn't handle non-finite values.
Results may differ from a plain program's by a relative error of at most 0.0066.
Values may be sent and summed in bfloat16 or wider, within the bound.
No kernel may reach another device: no remote copies, remote signals or barrier semaphores. Data moves between devices by JAX's collectives and lax.ppermute only.
A program may use at most 64 MiB of HBM per device.

v0:
```python
import jax
import jax.numpy as jnp
from jax import lax
from jax.sharding import PartitionSpec as P


def with_halo(block, sides, width):
    for axis, dim in sides:
        count = lax.axis_size(axis)
        forward = [(i, i + 1) for i in range(count - 1)]
        backward = [(target, source) for source, target in forward]
        low = lax.ppermute(
            lax.slice_in_dim(block, block.shape[dim] - width, None, axis=dim), axis, forward
        )
        high = lax.ppermute(lax.slice_in_dim(block, 0, width, axis=dim), axis, backward)
        block = jnp.concatenate([low, block, high], axis=dim)
    return block


def body(
    density,
    basis,
    near_list,
    near_blocks,
    far_leaf,
    leaf_coupling,
    transfer,
    far_coarse,
    coarse_coupling,
):
    leaf_count, rhs_count, leaf_width = density.shape
    rank_width = basis.shape[1]
    box_count = transfer.shape[0]
    child_count = leaf_count // box_count
    far_count = far_leaf.shape[1]
    coarse_count = far_coarse.shape[1]
    skeleton = jnp.einsum(
        "lrp,lkp->lrk", density, basis, preferred_element_type=jnp.float32
    ).astype(jnp.bfloat16)
    children = skeleton.reshape(box_count, child_count, rhs_count, rank_width)
    coarse = jnp.einsum(
        "ckim,cirm->crk",
        transfer.reshape(box_count, rank_width, child_count, rank_width),
        children,
        preferred_element_type=jnp.float32,
    ).astype(jnp.bfloat16)
    coarse_flat = coarse.reshape(box_count, rhs_count * rank_width)
    everything = lax.all_gather(coarse_flat, ("wide", "narrow"), axis=0, tiled=True)
    offset_base = lax.axis_index(("wide", "narrow")) * leaf_count - leaf_count
    density_flat = density.reshape(leaf_count, rhs_count * leaf_width)
    skeleton_flat = skeleton.reshape(leaf_count, rhs_count * rank_width)
    density_padded = with_halo(density_flat, ((("wide", "narrow"), 0),), leaf_count)
    skeleton_padded = with_halo(skeleton_flat, ((("wide", "narrow"), 0),), leaf_count)
    near_rows = jnp.take(density_padded, near_list - offset_base, axis=0).reshape(
        leaf_count, near_list.shape[1], rhs_count, leaf_width
    )
    near_part = jnp.einsum(
        "ljpq,ljrq->lrp", near_blocks, near_rows, preferred_element_type=jnp.float32
    )
    far_skels = jnp.take(skeleton_padded, far_leaf - offset_base, axis=0).reshape(
        leaf_count, far_count, rhs_count, rank_width
    )
    leaf_far = jnp.einsum(
        "lkjm,ljrm->lrk",
        leaf_coupling.reshape(leaf_count, rank_width, far_count, rank_width),
        far_skels,
        preferred_element_type=jnp.float32,
    )
    coarse_skels = jnp.take(everything, far_coarse, axis=0).reshape(
        box_count, coarse_count, rhs_count, rank_width
    )
    coarse_field = jnp.einsum(
        "ckjm,cjrm->crk",
        coarse_coupling.reshape(box_count, rank_width, coarse_count, rank_width),
        coarse_skels,
        preferred_element_type=jnp.float32,
    ).astype(jnp.bfloat16)
    descended = jnp.einsum(
        "ckim,crk->cirm",
        transfer.reshape(box_count, rank_width, child_count, rank_width),
        coarse_field,
        preferred_element_type=jnp.float32,
    ).reshape(leaf_count, rhs_count, rank_width)
    local_field = (leaf_far + descended).astype(jnp.bfloat16)
    total = (
        jnp.einsum("lrk,lkp->lrp", local_field, basis, preferred_element_type=jnp.float32)
        + near_part
    )
    return total.astype(jnp.bfloat16)


def solution(mesh):
    return jax.shard_map(
        body,
        mesh=mesh,
        in_specs=(
            P(("wide", "narrow"), None, None),
            P(("wide", "narrow"), None, None),
            P(("wide", "narrow"), None),
            P(("wide", "narrow"), None, None, None),
            P(("wide", "narrow"), None),
            P(("wide", "narrow"), None, None),
            P(("wide", "narrow"), None, None),
            P(("wide", "narrow"), None),
            P(("wide", "narrow"), None, None),
        ),
        out_specs=P(("wide", "narrow"), None, None),
        check_vma=False,
    )
```

profile of v0, /device:TPU:1, one launch (start us, length us, event | category | flops | bytes accessed | tf_op | source)
XLA Modules:
  0.0 415.8 jit_solution(6221959910823239641)
XLA Ops:
  6.5 0.0 copy-start
  6.5 0.0 copy-start.1
  6.5 0.0 all-gather.3.cloned.1.call-start
  6.5 1.4 reshape.49
  8.0 0.0 copy-done
  8.0 1.2 convolution_convert_fusion
  9.2 0.3 fusion.16
  9.4 0.7 reshape.87
  10.1 0.0 all-gather.3.cloned.1.call-update
  10.2 0.1 reshape.46
  10.3 6.2 %collective-permute-start = (bf16[32,512]{1,0:T(8,128)(2,1)S(1)}, bf16[32,512]{1,0:T(8,128)(2,1)S(1)}, u32[]{:S(2)}, u32[]{:S(2)}) collective-permute-start(bf16[32,512]{1,0:T(8,128)(2,1)S(1)} %reshape.46), channel_id=1, source_target_pairs={{0,1},{1,2},{2,3},{3,4},{4,5},{5,6},{6,7},{7,8},{8,9},{9,10},{10,1... | collective-permute-start | bytes 98312 | tf_op jit(solution)/shard_map/ppermute | solution.py:12
  16.5 1.9 collective-permute-start.1
  18.4 0.9 copy.53
  19.3 5.1 %collective-permute-start.2 = (bf16[32,1024]{1,0:T(8,128)(2,1)S(1)}, bf16[32,1024]{1,0:T(8,128)(2,1)S(1)}, u32[]{:S(2)}, u32[]{:S(2)}) collective-permute-start(bf16[32,1024]{1,0:T(8,128)(2,1)S(1)} %bitcast.57), channel_id=1, source_target_pairs={{0,1},{1,2},{2,3},{3,4},{4,5},{5,6},{6,7},{7,8},{8,9},{9,10},{10,1... | collective-permute-start | bytes 196616 | tf_op jit(solution)/shard_map/ppermute | solution.py:12
  24.4 1.9 collective-permute-start.3
  26.4 0.7 compare_and_fusion
  27.1 0.1 copy.21
  27.2 0.1 reshape.56
  27.3 0.7 compare_select_fusion.2
  27.9 0.1 reshape.64
  28.0 0.1 copy.27
  28.1 0.1 reshape.72
  28.3 0.7 compare_and_fusion.2
  29.0 0.1 copy.20
  29.1 1.3 reshape.51
  30.3 0.0 copy-done.1
  30.3 3.7 reshape.47
  34.1 0.1 copy.26
  34.2 0.0 collective-permute-done
  34.2 0.0 collective-permute-done.1
  34.2 1.0 gather_fusion
  35.2 0.2 gather.19
  35.4 0.0 collective-permute-done.2
  35.5 0.0 collective-permute-done.3
  35.5 1.0 gather_fusion.2
  36.5 0.1 copy.34
  36.6 361.3 %all-gather.3.cloned.1.call-done = bf16[256,4,512]{2,1,0:T(4,128)(2,1)} async-done(((bf16[1,4,512]{2,1,0:T(4,128)(2,1)}), bf16[256,4,512]{2,1,0:T(4,128)(2,1)}) %all-gather.3.cloned.1.call-update) | async-done | bytes 1048592 | tf_op jit(solution)/shard_map/all_gather | solution.py:48
  397.9 1.3 reshape.88
  399.2 0.6 gather_fusion.1
  399.8 0.1 gather.21
  399.9 0.4 fusion.19
  400.4 3.4 fusion.14
  403.8 5.2 %fusion.12 = bf16[32,8,128]{2,1,0:T(8,128)(2,1)} fusion(f32[32,8,128]{2,1,0:T(8,128)S(1)} %fusion.14, bf16[32,6,128,128]{3,2,1,0:T(8,128)(2,1)} %param.12, bf16[32,6,8,128]{3,2,1,0:T(8,128)(2,1)S(1)} %bitcast.53, pred[32,6]{1,0:T(8,128)(4,1)S(1)} %copy.26), kind=kOutput, calls=%fused_computation.10 | convolution fusion | flops 50593792 | bytes 6881472 | tf_op jit(solution)/shard_map/ljpq,ljrq->lrp/dot_general | solution.py:57
  (5 shorter events, 0.0 us)
Async XLA Ops:
  6.5 1.4 copy-start
  6.5 23.8 %copy-start.1 = (bf16[32,64,384]{2,1,0:T(8,128)(2,1)S(1)}, bf16[32,64,384]{2,1,0:T(8,128)(2,1)}, u32[]{:S(2)}) copy-start(bf16[32,64,384]{2,1,0:T(8,128)(2,1)} %param.14) | copy-start | bytes 4718596
  6.5 391.3 %all-gather.3.cloned.1.call-start = ((), (), s32[]{:S(2)}) async-start(), calls=%async_computation | async-start | bytes 1052672 | tf_op jit(solution)/shard_map/all_gather | solution.py:48
  10.3 23.9 %collective-permute-start = (bf16[32,512]{1,0:T(8,128)(2,1)S(1)}, bf16[32,512]{1,0:T(8,128)(2,1)S(1)}, u32[]{:S(2)}, u32[]{:S(2)}) collective-permute-start(bf16[32,512]{1,0:T(8,128)(2,1)S(1)} %reshape.46), channel_id=1, source_target_pairs={{0,1},{1,2},{2,3},{3,4},{4,5},{5,6},{6,7},{7,8},{8,9},{9,10},{10,1... | collective-permute-start | bytes 98312 | tf_op jit(solution)/shard_map/ppermute | solution.py:12
  16.5 17.7 %collective-permute-start.1 = (bf16[32,512]{1,0:T(8,128)(2,1)S(1)}, bf16[32,512]{1,0:T(8,128)(2,1)S(1)}, u32[]{:S(2)}, u32[]{:S(2)}) collective-permute-start(bf16[32,512]{1,0:T(8,128)(2,1)S(1)} %reshape.46), channel_id=1, source_target_pairs={{1,0},{2,1},{3,2},{4,3},{5,4},{6,5},{7,6},{8,7},{9,8},{10,9},{11,1... | collective-permute-start | bytes 98312 | tf_op jit(solution)/shard_map/ppermute | solution.py:15
  19.3 16.2 %collective-permute-start.2 = (bf16[32,1024]{1,0:T(8,128)(2,1)S(1)}, bf16[32,1024]{1,0:T(8,128)(2,1)S(1)}, u32[]{:S(2)}, u32[]{:S(2)}) collective-permute-start(bf16[32,1024]{1,0:T(8,128)(2,1)S(1)} %bitcast.57), channel_id=1, source_target_pairs={{0,1},{1,2},{2,3},{3,4},{4,5},{5,6},{6,7},{7,8},{8,9},{9,10},{10,1... | collective-permute-start | bytes 196616 | tf_op jit(solution)/shard_map/ppermute | solution.py:12
  24.4 11.0 %collective-permute-start.3 = (bf16[32,1024]{1,0:T(8,128)(2,1)S(1)}, bf16[32,1024]{1,0:T(8,128)(2,1)S(1)}, u32[]{:S(2)}, u32[]{:S(2)}) collective-permute-start(bf16[32,1024]{1,0:T(8,128)(2,1)S(1)} %bitcast.58), channel_id=1, source_target_pairs={{1,0},{2,1},{3,2},{4,3},{5,4},{6,5},{7,6},{8,7},{9,8},{10,9},{11,1... | collective-permute-start | bytes 196616 | tf_op jit(solution)/shard_map/ppermute | solution.py:15
Sparse Core Ops, SparseCore 0:
  10.3 387.5 all-gather.2
where the time goes:
time: 416 us
  waiting for transfers between devices  361 us (87%)
  starting transfers between devices  15.2 us (4%)
  between operations  13.6 us (3%)
  local copies, waits for them, and re-layouts  13.1 us (3%)
  matrix products  10.5 us (3%)
    all_gather x1, waiting for transfers between devices, body(): lax.all_gather(coarse_flat, ('wide', 'narrow'), axis=0, tiled=True)  361 us
    ppermute x2, starting transfers between devices, with_halo(): lax.ppermute(lax.slice_in_dim(block, block.shape[dim] - width, None, axis...  11.3 us
  transfers between devices with their start and end apart: 5, of which 1 were waited for; matrix products, arithmetic and copies ran while one was open for 3% of the time, Pallas kernels for 0%

commit v1 on v0

--- a/solution.py
+++ b/solution.py
@@ -2,6 +2,7 @@
 import jax.numpy as jnp
 from jax import lax
 from jax.sharding import PartitionSpec as P
+from jax.lax import all_to_all, axis_size
 
 
 def with_halo(block, sides, width):
@@ -45,7 +46,15 @@
         preferred_element_type=jnp.float32,
     ).astype(jnp.bfloat16)
     coarse_flat = coarse.reshape(box_count, rhs_count * rank_width)
-    everything = lax.all_gather(coarse_flat, ("wide", "narrow"), axis=0, tiled=True)
+    everything = jnp.concatenate(
+        all_to_all(
+            jnp.stack(axis_size(("wide", "narrow")) * [coarse_flat], axis=0),
+            ("wide", "narrow"),
+            0,
+            0,
+        ),
+        0,
+    )
     offset_base = lax.axis_index(("wide", "narrow")) * leaf_count - leaf_count
     density_flat = density.reshape(leaf_count, rhs_count * leaf_width)
     skeleton_flat = skeleton.reshape(leaf_count, rhs_count * rank_width)

time: 416 us -> 63.4 us (0.15)
  waiting for transfers between devices: 361 us -> 7.64 us
  starting transfers between devices: 15.2 us -> 29.7 us
  between operations: 13.6 us -> 0.23 us
    all_gather x1 -> x0, waiting for transfers between devices: 361 us -> none  [body(): lax.all_gather(coarse_flat, ('wide', 'narrow'), axis=0, tiled=True)]
    all_to_all x0 -> x1, starting transfers between devices: none -> 15.6 us  [body(): all_to_all(jnp.stack(axis_size(('wide', 'narrow')) * [coarse_flat], axis=...]
    all_to_all x0 -> x1, waiting for transfers between devices: none -> 7.63 us  [body(): all_to_all(jnp.stack(axis_size(('wide', 'narrow')) * [coarse_flat], axis=...]
  transfers between devices with their start and end apart: 5 -> 5, of which waited for: 1 -> 1; matrix products, arithmetic and copies ran while one was open for 3% -> 15% of each run, Pallas kernels for 0% -> 0%
where the time goes in v1:
time: 63.4 us; the launch traced here: 63 us
  starting transfers between devices  29.7 us (47%)
  local copies, waits for them, and re-layouts  15.1 us (24%)
  matrix products  10.2 us (16%)
  waiting for transfers between devices  7.64 us (12%)
    all_to_all x1, starting transfers between devices, body(): all_to_all(jnp.stack(axis_size(('wide', 'narrow')) * [coarse_flat], axis=...  15.6 us
    ppermute x2, starting transfers between devices, with_halo(): lax.ppermute(lax.slice_in_dim(block, block.shape[dim] - width, None, axis...  10.2 us
    all_to_all x1, waiting for transfers between devices, body(): all_to_all(jnp.stack(axis_size(('wide', 'narrow')) * [coarse_flat], axis=...  7.63 us
    dot_general x1, matrix products, body(): jnp.einsum('ljpq,ljrq->lrp', near_blocks, near_rows, preferred_element_ty...  5.2 us
    reshape x1, local copies, waits for them, and re-layouts, body(): leaf_coupling.reshape(leaf_count, rank_width, far_count, rank_width)  4.18 us
    ppermute x2, starting transfers between devices, with_halo(): lax.ppermute(lax.slice_in_dim(block, 0, width, axis=dim), axis, backward)  3.84 us
    dot_general x1, matrix products, body(): jnp.einsum('lrk,lkp->lrp', local_field, basis, preferred_element_type=jnp...  3.09 us
    gather x2, local copies, waits for them, and re-layouts, body(): jnp.take(everything, far_coarse, axis=0)  2.14 us
  transfers between devices with their start and end apart: 5, of which 1 were waited for; matrix products, arithmetic and copies ran while one was open for 15% of the time, Pallas kernels for 0%

profile of v1, /device:TPU:1, one launch (start us, length us, event | category | flops | bytes accessed | tf_op | source)
XLA Modules:
  0.0 63.0 jit_solution(6943628366080971511)
XLA Ops:
  0.0 0.0 copy-start
  0.0 0.0 copy-start.4
  0.0 0.0 copy-start.6
  0.0 0.0 copy-start.7
  0.0 0.0 copy-start.5
  0.0 0.0 copy-start.3
  0.0 1.3 %reshape.51 = bf16[4,64,8,64]{3,2,1,0:T(8,128)(2,1)S(1)} reshape(bf16[4,64,512]{2,1,0:T(8,128)(2,1)} %param.15) | data formatting | bytes 524288 | tf_op jit(solution)/shard_map/reshape | solution.py:44
  1.4 0.0 copy-done
  1.4 1.2 %convolution_convert_fusion = bf16[32,8,64]{2,1,0:T(8,128)(2,1)S(1)} fusion(bf16[32,8,128]{2,1,0:T(8,128)(2,1)} %param.9, bf16[32,64,128]{2,1,0:T(8,128)(2,1)S(1)} %copy-done), kind=kOutput, calls=%fused_computation.9 | convolution fusion | flops 4210688 | bytes 622592 | tf_op jit(solution)/shard_map/lrp,lkp->lrk/dot_general | solution.py:38
  2.6 0.3 fusion.5
  2.9 0.1 stack_reshape.2
  2.9 1.3 %stack.3 = bf16[256,4,512]{2,1,0:T(4,128)(2,1)} broadcast(bf16[4,512]{1,0:T(4,128)(2,1)S(1)} %stack_reshape.2), dimensions={1,2} | broadcast | bytes 1052672 | tf_op jit(solution)/shard_map/stack | solution.py:51
  4.2 15.6 %all-to-all-start = ((bf16[256,4,512]{2,1,0:T(4,128)(2,1)}), bf16[256,4,512]{2,1,0:T(4,128)(2,1)S(1)}, u32[]{:S(2)}, u32[]{:S(2)}) async-start(bf16[256,4,512]{2,1,0:T(4,128)(2,1)} %stack.3), calls=%async_computation | async-start | bytes 2097152 | tf_op jit(solution)/shard_map/all_to_all | solution.py:50
  19.9 0.1 reshape.48
  20.0 5.0 %collective-permute-start = (bf16[32,512]{1,0:T(8,128)(2,1)S(1)}, bf16[32,512]{1,0:T(8,128)(2,1)S(1)}, u32[]{:S(2)}, u32[]{:S(2)}) collective-permute-start(bf16[32,512]{1,0:T(8,128)(2,1)S(1)} %reshape.48), channel_id=1, source_target_pairs={{0,1},{1,2},{2,3},{3,4},{4,5},{5,6},{6,7},{7,8},{8,9},{9,10},{10,1... | collective-permute-start | bytes 98312 | tf_op jit(solution)/shard_map/ppermute | solution.py:13
  25.1 1.9 %collective-permute-start.1 = (bf16[32,512]{1,0:T(8,128)(2,1)S(1)}, bf16[32,512]{1,0:T(8,128)(2,1)S(1)}, u32[]{:S(2)}, u32[]{:S(2)}) collective-permute-start(bf16[32,512]{1,0:T(8,128)(2,1)S(1)} %reshape.48), channel_id=1, source_target_pairs={{1,0},{2,1},{3,2},{4,3},{5,4},{6,5},{7,6},{8,7},{9,8},{10,9},{11,1... | collective-permute-start | bytes 98312 | tf_op jit(solution)/shard_map/ppermute | solution.py:16
  27.0 0.0 copy-done.4
  27.0 5.1 %collective-permute-start.2 = (bf16[32,1024]{1,0:T(8,128)(2,1)S(1)}, bf16[32,1024]{1,0:T(8,128)(2,1)S(1)}, u32[]{:S(2)}, u32[]{:S(2)}) collective-permute-start(bf16[32,1024]{1,0:T(8,128)(2,1)S(1)} %bitcast.63), channel_id=1, source_target_pairs={{0,1},{1,2},{2,3},{3,4},{4,5},{5,6},{6,7},{7,8},{8,9},{9,10},{10,1... | collective-permute-start | bytes 196616 | tf_op jit(solution)/shard_map/ppermute | solution.py:13
  32.2 1.9 %collective-permute-start.3 = (bf16[32,1024]{1,0:T(8,128)(2,1)S(1)}, bf16[32,1024]{1,0:T(8,128)(2,1)S(1)}, u32[]{:S(2)}, u32[]{:S(2)}) collective-permute-start(bf16[32,1024]{1,0:T(8,128)(2,1)S(1)} %bitcast.64), channel_id=1, source_target_pairs={{1,0},{2,1},{3,2},{4,3},{5,4},{6,5},{7,6},{8,7},{9,8},{10,9},{11,1... | collective-permute-start | bytes 196616 | tf_op jit(solution)/shard_map/ppermute | solution.py:16
  34.1 0.0 copy-done.6
  34.1 0.0 copy-done.7
  34.1 0.1 copy.15
  34.2 0.1 reshape.58
  34.3 0.0 copy-done.5
  34.4 0.1 reshape.66
  34.4 0.1 copy.19
  34.5 0.1 reshape.74
  34.7 0.1 copy.14
  34.8 0.0 copy-done.3
  34.8 0.3 copy.28
  35.1 4.2 %copy.27 = bf16[32,64,384]{1,2,0:T(8,128)(2,1)} copy(bf16[32,64,384]{2,1,0:T(8,128)(2,1)} %param.14) | data formatting | bytes 3145728 | tf_op jit(solution)/shard_map/reshape | solution.py:74
  39.3 0.1 copy.18
  39.4 0.0 collective-permute-done
  39.4 0.0 collective-permute-done.1
  39.4 1.0 %gather_fusion = bf16[192,512]{1,0:T(8,128)(2,1)S(1)} fusion(bf16[96,512]{1,0:T(8,128)(2,1)S(1)} %pad_maximum_fusion.1, s32[1024]{0:T(1024)S(1)} %pad_clamp_fusion.2), kind=kCustom, calls=%fused_computation | custom fusion | bytes 393984 | tf_op jit(solution)/shard_map/jit(_take)/gather | solution.py:69
  40.4 1.0 %gather.19 = bf16[32,6,8,64]{3,2,1,0:T(8,128)(2,1)} reshape(bf16[192,512]{1,0:T(8,128)(2,1)S(1)} %gather_fusion) | data formatting | bytes 393216 | tf_op jit(solution)/shard_map/jit(_take)/gather | solution.py:69
  41.4 0.0 collective-permute-done.2
  41.4 0.0 collective-permute-done.3
  41.4 1.0 %gather_fusion.2 = bf16[192,1024]{1,0:T(8,128)(2,1)S(1)} fusion(bf16[96,1024]{1,0:T(8,128)(2,1)S(1)} %pad_maximum_fusion, s32[1024]{0:T(1024)S(1)} %pad_clamp_fusion), kind=kCustom, calls=%fused_computation.2 | custom fusion | bytes 787200 | tf_op jit(solution)/shard_map/jit(_take)/gather | solution.py:63
  42.5 0.0 copy-start.1
  42.5 0.8 %copy.30 = bf16[24,8,8,128]{3,2,1,0:T(8,128)(2,1)} copy(bf16[24,8,8,128]{3,1,2,0:T(8,128)(2,1)S(1)} %bitcast.57) | data formatting | bytes 786432
  43.3 7.6 %all-to-all-done = bf16[256,4,512]{2,1,0:T(4,128)(2,1)S(1)} async-done(((bf16[256,4,512]{2,1,0:T(4,128)(2,1)}), bf16[256,4,512]{2,1,0:T(4,128)(2,1)S(1)}, u32[]{:S(2)}, u32[]{:S(2)}) %all-to-all-start) | async-done | bytes 1048608 | tf_op jit(solution)/shard_map/all_to_all | solution.py:50
  50.9 1.1 %reshape.52 = bf16[1024,512]{1,0:T(8,128)(2,1)} reshape(bf16[256,4,512]{2,1,0:T(4,128)(2,1)S(1)} %all-to-all-done) | data formatting | bytes 2097152 | tf_op jit(solution)/shard_map/reshape | solution.py:49
  52.1 0.0 copy-start.2
  52.1 2.0 %gather_fusion.1 = bf16[32,512]{1,0:T(8,128)(2,1)S(1)} fusion(bf16[1024,512]{1,0:T(8,128)(2,1)} %reshape.52, s32[1024]{0:T(1024)S(1)} %pad_clamp_fusion.1), kind=kCustom, calls=%fused_computation.1 | custom fusion | bytes 65664 | tf_op jit(solution)/shard_map/jit(_take)/gather | solution.py:78
  54.1 0.1 gather.21
  54.2 0.5 fusion.8
  54.7 0.0 copy-done.1
  54.7 3.1 %fusion.4 = f32[32,8,128]{2,1,0:T(8,128)S(1)} fusion(bf16[32,64,128]{2,1,0:T(8,128)(2,1)S(1)} %copy-done, f32[32,8,64]{2,1,0:T(8,128)S(1)} %bitcast.61, bf16[32,64,6,64]{1,3,2,0:T(8,128)(2,1)} %bitcast.56, bf16[32,6,8,64]{3,2,1,0:T(8,128)(2,1)S(1)} %copy-done.1, pred[32,6]{1,0:T(8,128)(4,1)S(1)} %copy.14), kind=kOutput, calls=%fused_computation.10 | convolution fusion | flops 16908288 | bytes 2490560 | tf_op jit(solution)/shard_map/lrk,lkp->lrp/dot_general | solution.py:95
  57.8 0.0 copy-done.2
  57.8 5.2 %fusion.3 = bf16[32,8,128]{2,1,0:T(8,128)(2,1)} fusion(f32[32,8,128]{2,1,0:T(8,128)S(1)} %fusion.4, bf16[32,6,128,128]{3,2,1,0:T(8,128)(2,1)} %param.12, bf16[32,6,8,128]{3,2,1,0:T(8,128)(2,1)S(1)} %bitcast.59, pred[32,6]{1,0:T(8,128)(4,1)S(1)} %copy.18), kind=kOutput, calls=%fused_computation.8 | convolution fusion | flops 50593792 | bytes 6881472 | tf_op jit(solution)/shard_map/ljpq,ljrq->lrp/dot_general | solution.py:66
  (9 shorter events, 0.1 us)
Async XLA Ops:
  0.0 1.4 %copy-start = (bf16[32,64,128]{2,1,0:T(8,128)(2,1)S(1)}, bf16[32,64,128]{2,1,0:T(8,128)(2,1)}, u32[]{:S(2)}) copy-start(bf16[32,64,128]{2,1,0:T(8,128)(2,1)} %param.10) | copy-start | bytes 1572868
  0.0 27.0 %copy-start.4 = (bf16[32,8,128]{2,1,0:T(8,128)(2,1)S(1)}, bf16[32,8,128]{2,1,0:T(8,128)(2,1)}, u32[]{:S(2)}) copy-start(bf16[32,8,128]{2,1,0:T(8,128)(2,1)} %param.9) | copy-start | bytes 196612
  0.0 34.1 %copy-start.6 = (s32[32,6]{0,1:T(8,128)S(1)}, s32[32,6]{0,1:T(8,128)}, u32[]{:S(2)}) copy-start(s32[32,6]{0,1:T(8,128)} %param.11) | copy-start | bytes 2308
  0.0 34.1 %copy-start.7 = (s32[32,6]{0,1:T(8,128)S(1)}, s32[32,6]{0,1:T(8,128)}, u32[]{:S(2)}) copy-start(s32[32,6]{0,1:T(8,128)} %param.13) | copy-start | bytes 2308
  0.0 34.3 %copy-start.5 = (s32[4,8]{1,0:T(4,128)S(1)}, s32[4,8]{1,0:T(4,128)}, u32[]{:S(2)}) copy-start(s32[4,8]{1,0:T(4,128)} %param.16) | copy-start | bytes 388
  0.0 34.8 %copy-start.3 = (bf16[4,64,512]{2,1,0:T(8,128)(2,1)S(1)}, bf16[4,64,512]{2,1,0:T(8,128)(2,1)}, u32[]{:S(2)}) copy-start(bf16[4,64,512]{2,1,0:T(8,128)(2,1)} %param.17) | copy-start | bytes 786436
  4.2 46.7 %all-to-all-start = ((bf16[256,4,512]{2,1,0:T(4,128)(2,1)}), bf16[256,4,512]{2,1,0:T(4,128)(2,1)S(1)}, u32[]{:S(2)}, u32[]{:S(2)}) async-start(bf16[256,4,512]{2,1,0:T(4,128)(2,1)} %stack.3), calls=%async_computation | async-start | bytes 2097152 | tf_op jit(solution)/shard_map/all_to_all | solution.py:50
  20.0 19.4 %collective-permute-start = (bf16[32,512]{1,0:T(8,128)(2,1)S(1)}, bf16[32,512]{1,0:T(8,128)(2,1)S(1)}, u32[]{:S(2)}, u32[]{:S(2)}) collective-permute-start(bf16[32,512]{1,0:T(8,128)(2,1)S(1)} %reshape.48), channel_id=1, source_target_pairs={{0,1},{1,2},{2,3},{3,4},{4,5},{5,6},{6,7},{7,8},{8,9},{9,10},{10,1... | collective-permute-start | bytes 98312 | tf_op jit(solution)/shard_map/ppermute | solution.py:13
  25.1 14.3 %collective-permute-start.1 = (bf16[32,512]{1,0:T(8,128)(2,1)S(1)}, bf16[32,512]{1,0:T(8,128)(2,1)S(1)}, u32[]{:S(2)}, u32[]{:S(2)}) collective-permute-start(bf16[32,512]{1,0:T(8,128)(2,1)S(1)} %reshape.48), channel_id=1, source_target_pairs={{1,0},{2,1},{3,2},{4,3},{5,4},{6,5},{7,6},{8,7},{9,8},{10,9},{11,1... | collective-permute-start | bytes 98312 | tf_op jit(solution)/shard_map/ppermute | solution.py:16
  27.0 14.4 %collective-permute-start.2 = (bf16[32,1024]{1,0:T(8,128)(2,1)S(1)}, bf16[32,1024]{1,0:T(8,128)(2,1)S(1)}, u32[]{:S(2)}, u32[]{:S(2)}) collective-permute-start(bf16[32,1024]{1,0:T(8,128)(2,1)S(1)} %bitcast.63), channel_id=1, source_target_pairs={{0,1},{1,2},{2,3},{3,4},{4,5},{5,6},{6,7},{7,8},{8,9},{9,10},{10,1... | collective-permute-start | bytes 196616 | tf_op jit(solution)/shard_map/ppermute | solution.py:13
  32.2 9.3 %collective-permute-start.3 = (bf16[32,1024]{1,0:T(8,128)(2,1)S(1)}, bf16[32,1024]{1,0:T(8,128)(2,1)S(1)}, u32[]{:S(2)}, u32[]{:S(2)}) collective-permute-start(bf16[32,1024]{1,0:T(8,128)(2,1)S(1)} %bitcast.64), channel_id=1, source_target_pairs={{1,0},{2,1},{3,2},{4,3},{5,4},{6,5},{7,6},{8,7},{9,8},{10,9},{11,1... | collective-permute-start | bytes 196616 | tf_op jit(solution)/shard_map/ppermute | solution.py:16
  42.5 12.2 %copy-start.1 = (bf16[32,6,8,64]{3,2,1,0:T(8,128)(2,1)S(1)}, bf16[32,6,8,64]{3,2,1,0:T(8,128)(2,1)}, u32[]{:S(2)}) copy-start(bf16[32,6,8,64]{3,2,1,0:T(8,128)(2,1)} %gather.19) | copy-start | bytes 589828
  52.1 5.7 %copy-start.2 = (bf16[24,8,8,128]{3,2,1,0:T(8,128)(2,1)S(1)}, bf16[24,8,8,128]{3,2,1,0:T(8,128)(2,1)}, u32[]{:S(2)}) copy-start(bf16[24,8,8,128]{3,2,1,0:T(8,128)(2,1)} %copy.30) | copy-start | bytes 1179652
